TPU v7x, 32 devices: a whole 2x2x4 slice. The times are simulated.
32 devices in a mesh: ctx: 8 (over y, x, core), mp: 4 (over z).
Axes of the slice: x: 2, y: 2, z: 4, core: 2. Of those that a mesh axis runs over, the one named last changes fastest.
Arguments:
- cotangent: bfloat16 [1536, 8192], P('ctx', 'mp'), may hold values from -6 to 6
- out_weight: bfloat16 [8192, 8192], P('mp', 'ctx'), may hold values from -0.0625 to 0.0625
- query_act: bfloat16 [1536, 8192], P('ctx', 'mp'), may hold values from -6 to 6
- key_act: bfloat16 [1536, 8192], P('ctx', 'mp'), may hold values from -6 to 6
- value_act: bfloat16 [1536, 8192], P('ctx', 'mp'), may hold values from -6 to 6
- filters: float32 [512, 128], replicated, may hold values from -0.5 to 0.5
Outputs:
- grad_query: bfloat16 [1536, 8192], P('ctx', 'mp')
- grad_key: bfloat16 [1536, 8192], P('ctx', 'mp')
- grad_value: bfloat16 [1536, 8192], P('ctx', 'mp')
- grad_filters: float32 [512, 128], replicated
All inputs are finite; a program needn't handle non-finite values.
Results may differ from a plain program's by a relative error of at most 0.0051.
Values may be sent and summed in bfloat16 or wider, within the bound.
No kernel may reach another device: no remote copies, remote signals or barrier semaphores. Data moves between devices by JAX's collectives and lax.ppermute only.
A program may use at most 128 MiB of HBM per device.

v0:
```python
import jax
import jax.numpy as jnp
from jax import lax
from jax.sharding import PartitionSpec as P


def causal(widened, taps, rows, prev):

    def causal_step(shift, total):
        window = lax.dynamic_slice_in_dim(widened, (prev - shift).astype(jnp.int32), rows, 0)
        weight = lax.dynamic_slice_in_dim(taps, shift.astype(jnp.int32), 1, 0)
        return total + weight * window

    return lax.fori_loop(
        jnp.int32(0),
        jnp.int32(prev + 1),
        causal_step,
        jnp.zeros((rows, widened.shape[1]), widened.dtype),
    )


def anticausal(trailing, taps, rows, prev):

    def anticausal_step(shift, total):
        window = lax.dynamic_slice_in_dim(trailing, shift.astype(jnp.int32), rows, 0)
        weight = lax.dynamic_slice_in_dim(taps, shift.astype(jnp.int32), 1, 0)
        return total + weight * window

    return lax.fori_loop(
        jnp.int32(0),
        jnp.int32(prev + 1),
        anticausal_step,
        jnp.zeros((rows, trailing.shape[1]), trailing.dtype),
    )


def lagged(widened, gradient, prev):
    rows = gradient.shape[0]

    def one_lag(shift):
        window = lax.dynamic_slice_in_dim(widened, prev - shift, rows, 0)
        return jnp.sum(window * gradient, axis=0)

    return lax.map(one_lag, jnp.arange(prev + 1, dtype=jnp.int32))


def contract(left, right):
    return lax.dot_general(
        left, right, (((1,), (1,)), ((), ())), preferred_element_type=jnp.float32
    )


def group_table(first, count, per_group, groups):
    channel = first + jnp.arange(count)
    return (channel[None, :] // per_group == jnp.arange(groups)[:, None]).astype(jnp.float32)


def body(cotangent, out_weight, query_act, key_act, value_act, filters):
    tok_rows, chans = cotangent.shape
    groups, taps_len = filters.shape
    prev = taps_len - 1
    ctx_count = lax.axis_size("ctx")
    per_group = chans * lax.axis_size("mp") // groups
    panel = lax.all_gather(out_weight, "ctx", axis=1, tiled=True)
    grad_mixed = contract(lax.all_gather(cotangent, "mp", axis=1, tiled=True), panel)
    product = (key_act.astype(jnp.float32) * value_act.astype(jnp.float32)).astype(jnp.bfloat16)
    grad_conv = (grad_mixed * query_act.astype(jnp.float32)).astype(jnp.bfloat16)
    narrow = chans // ctx_count
    seq_product, seq_grad = (
        lax.all_to_all(product, "ctx", split_axis=1, concat_axis=0, tiled=True),
        lax.all_to_all(grad_conv, "ctx", split_axis=1, concat_axis=0, tiled=True),
    )
    onehot = group_table(
        lax.axis_index("mp") * chans + lax.axis_index("ctx") * narrow, narrow, per_group, groups
    )
    taps = jnp.dot(filters.T, onehot, precision=lax.Precision.HIGHEST)
    seq_rows = seq_grad.shape[0]
    grad_wide = seq_grad.astype(jnp.float32)
    widened = jnp.concatenate(
        [jnp.zeros((prev, narrow), jnp.float32), seq_product.astype(jnp.float32)], 0
    )
    trailing = jnp.concatenate([grad_wide, jnp.zeros((prev, narrow), jnp.float32)], 0)
    seq_mixed = causal(widened, taps, seq_rows, prev)
    seq_back = anticausal(trailing, taps, seq_rows, prev)
    corr = lagged(widened, grad_wide, prev)
    mixed, grad_product = (
        lax.all_to_all(seq_mixed, "ctx", split_axis=0, concat_axis=1, tiled=True),
        lax.all_to_all(seq_back, "ctx", split_axis=0, concat_axis=1, tiled=True),
    )
    grad_query = (grad_mixed * mixed).astype(jnp.bfloat16)
    grad_key = (grad_product * value_act.astype(jnp.float32)).astype(jnp.bfloat16)
    grad_value = (grad_product * key_act.astype(jnp.float32)).astype(jnp.bfloat16)
    partial_terms = jnp.dot(onehot, corr.T, precision=lax.Precision.HIGHEST)
    scale = (tok_rows * ctx_count * per_group) ** (-0.5)
    grad_filters = lax.psum(partial_terms, ("ctx", "mp")) * scale
    return (grad_query, grad_key, grad_value, grad_filters)


def solution(mesh):
    in_specs = (P("ctx", "mp"), P("mp", "ctx"), P("ctx", "mp"), P("ctx", "mp"), P("ctx", "mp"), P())
    out_specs = (P("ctx", "mp"), P("ctx", "mp"), P("ctx", "mp"), P())
    return jax.shard_map(body, mesh=mesh, in_specs=in_specs, out_specs=out_specs, check_vma=False)
```

profile of v0, /device:TPU:0, one launch (start us, length us, event | category | flops | bytes accessed | tf_op | source)
XLA Modules:
  0.0 1397.0 jit_solution(9679557478164837878)
XLA Ops:
  8.7 67.1 %all-gather.3.cloned.1.call-done = bf16[192,8192]{1,0:T(8,128)(2,1)} async-done(((bf16[192,2048]{1,0:T(8,128)(2,1)}), bf16[192,8192]{1,0:T(8,128)(2,1)}) %all-gather.3.cloned.1.call-update) | async-done | bytes 3145744 | tf_op jit(solution)/shard_map/all_gather | solution.py:65
  75.8 161.4 %all-gather.5.cloned.1.call-done = bf16[2048,8192]{1,0:T(8,128)(2,1)} async-done(((bf16[2048,1024]{1,0:T(8,128)(2,1)}), bf16[2048,8192]{1,0:T(8,128)(2,1)}) %all-gather.5.cloned.1.call-update) | async-done | bytes 33554448 | tf_op jit(solution)/shard_map/all_gather | solution.py:64
  237.2 18.0 %multiply_convert_fusion = (bf16[192,2048]{1,0:T(8,128)(2,1)S(1)}, f32[192,2048]{1,0:T(8,128)}) fusion(bf16[192,2048]{1,0:T(8,128)(2,1)S(1)} %copy-done.7, bf16[192,8192]{1,0:T(8,128)(2,1)} %all-gather.3.cloned.1.call-done, bf16[2048,8192]{1,0:T(8,128)(2,1)} %all-gather.5.cloned.1.call-done), kind=kOutput, calls=%fused_computation.11 | convolution fusion | flops 6443630592 | bytes 39845888 | tf_op jit(solution)/shard_map/dot_general | solution.py:48
  256.1 3.5 all-to-all-start.2
  260.5 11.8 all-to-all-done.2
  274.4 282.6 %while.38 = (s32[]{:T(128)}, f32[1536,256]{1,0:T(8,128)S(1)}, f32[128,256]{1,0:T(8,128)S(1)}, f32[1663,256]{1,0:T(8,128)}, s32[]{:T(128)}, /*index=5*/s32[]{:T(128)}) while((s32[]{:T(128)}, f32[1536,256]{1,0:T(8,128)S(1)}, f32[128,256]{1,0:T(8,128)S(1)}, f32[1663,256]{1,0:T(8,128)}, s32[]{:T(128)}, /*index=5*/s32[]{:T(128)}) %tuple.98), condition=%wide.region_3.4_spmd.clone, body=%wide.region_2.3_spmd.clone.sunk | while | flops 1179651 | bytes 4721759 | solution.py:29
  557.0 23.4 %all_to_all.64 = f32[8,192,256]{2,1,0:T(8,128)S(1)} all-to-all(f32[8,192,256]{2,1,0:T(8,128)S(1)} %bitcast.45), channel_id=1, replica_groups=mesh['ctx'=8,'mp'=4] {'ctx'}, dimensions={0} | all-to-all | bytes 3145728 | tf_op jit(solution)/shard_map/all_to_all | solution.py:88
  584.3 3.5 all-to-all-start
  587.9 12.5 all-to-all-done
  602.6 364.1 %while.37 = (s32[]{:T(128)}, f32[1536,256]{1,0:T(8,128)}, f32[128,256]{1,0:T(8,128)S(1)}, f32[1663,256]{1,0:T(8,128)S(1)}, s32[]{:T(128)}, /*index=5*/s32[]{:T(128)}, s32[]{:T(128)}, s32[]{:T(128)}) while((s32[]{:T(128)}, f32[1536,256]{1,0:T(8,128)}, f32[128,256]{1,0:T(8,128)S(1)}, f32[1663,256]{1,0:T(8,128)S(1)}, s32[]{:T(128)}, ...), condition=%wide.region_1.2_spmd.clone, body=%wide.region_0.1_spmd.clone.sunk | while | flops 1179655 | bytes 4721821 | solution.py:14
  604.1 2.9 select_add_fusion.4
  607.0 2.9 select_add_fusion.4
  609.9 2.9 select_add_fusion.4
  612.8 2.9 select_add_fusion.4
  615.7 2.9 select_add_fusion.4
  618.6 2.9 select_add_fusion.4
  621.5 2.9 select_add_fusion.4
  646.9 2.9 select_add_fusion.4
  649.8 2.9 select_add_fusion.4
  652.7 2.9 select_add_fusion.4
  655.6 2.9 select_add_fusion.4
  658.5 2.9 select_add_fusion.4
  661.4 2.9 select_add_fusion.4
  664.3 2.9 select_add_fusion.4
  667.2 2.9 select_add_fusion.4
  692.6 2.9 select_add_fusion.4
  695.5 2.9 select_add_fusion.4
  698.4 2.9 select_add_fusion.4
  701.3 2.9 select_add_fusion.4
  704.2 2.9 select_add_fusion.4
  707.1 2.9 select_add_fusion.4
  710.0 2.9 select_add_fusion.4
  712.9 2.9 select_add_fusion.4
  738.3 2.9 select_add_fusion.4
  741.2 2.9 select_add_fusion.4
  744.1 2.9 select_add_fusion.4
  747.0 2.9 select_add_fusion.4
  749.8 2.9 select_add_fusion.4
  752.7 2.9 select_add_fusion.4
  755.6 2.9 select_add_fusion.4
  758.5 2.9 select_add_fusion.4
  783.9 2.9 select_add_fusion.4
  789.7 2.9 select_add_fusion.4
  792.6 2.9 select_add_fusion.4
  801.3 2.9 select_add_fusion.4
  804.2 2.9 select_add_fusion.4
  829.6 2.9 select_add_fusion.4
  835.4 2.9 select_add_fusion.4
  838.3 2.9 select_add_fusion.4
  847.0 2.9 select_add_fusion.4
  849.9 2.9 select_add_fusion.4
  875.3 2.9 select_add_fusion.4
  881.1 2.9 select_add_fusion.4
  884.0 2.9 select_add_fusion.4
  892.7 2.9 select_add_fusion.4
  895.6 2.9 select_add_fusion.4
  921.0 2.9 select_add_fusion.4
  926.8 2.9 select_add_fusion.4
  929.7 2.9 select_add_fusion.4
  938.4 2.9 select_add_fusion.4
  941.3 2.9 select_add_fusion.4
  966.7 4.3 all-to-all-start.1
  971.0 287.3 %while.36 = (s32[]{:T(128)}, f32[128,256]{1,0:T(8,128)S(1)}, s32[128]{0:T(128)S(1)}, f32[1663,256]{1,0:T(8,128)S(1)}, f32[1536,256]{1,0:T(8,128)S(1)}, /*index=5*/s32[]{:T(128)}, s32[1]{0:T(128)}, s32[]{:T(128)}, s32[1]{0:T(128)}) while((s32[]{:T(128)}, f32[128,256]{1,0:T(8,128)S(1)}, s32[128]{0:T(128)S(1)}, f32[1663,256]{1,0:T(8,128)S(1)}, ...), condition=%wide.region_6.7_spmd, body=%wide.region_4.6_spmd.sunk | while | flops 786182 | bytes 3148967 | solution.py:44
  1259.5 126.4 %all-reduce.4.cloned.1.call-done = f32[512,128]{1,0:T(8,128)} async-done(((f32[512,128]{1,0:T(8,128)}), f32[512,128]{1,0:T(8,128)}) %all-reduce.4.cloned.1.call-update) | async-done | bytes 262160 | tf_op jit(solution)/shard_map/psum | solution.py:95
  (886 shorter events, 630.4 us)
Async XLA Ops:
  7.2 252.6 %copy-start = (f32[512,128]{1,0:T(8,128)S(1)}, f32[512,128]{1,0:T(8,128)}, u32[]{:S(2)}) copy-start(f32[512,128]{1,0:T(8,128)} %param.17) | copy-start | bytes 786436
  7.2 68.6 %all-gather.3.cloned.1.call-start = ((), (), s32[]{:S(2)}) async-start(), calls=%async_computation.4 | async-start | bytes 3932160 | tf_op jit(solution)/shard_map/all_gather | solution.py:65
  7.9 229.3 %copy-start.7 = (bf16[192,2048]{1,0:T(8,128)(2,1)S(1)}, bf16[192,2048]{1,0:T(8,128)(2,1)}, u32[]{:S(2)}) copy-start(bf16[192,2048]{1,0:T(8,128)(2,1)} %param.14) | copy-start | bytes 2359300
  7.9 229.3 %all-gather.5.cloned.1.call-start = ((), (), s32[]{:S(2)}) async-start(), calls=%async_computation.5 | async-start | bytes 37748736 | tf_op jit(solution)/shard_map/all_gather | solution.py:64
  256.1 16.1 %all-to-all-start.2 = ((bf16[192,8,256]{2,0,1:T(8,128)(2,1)}), bf16[192,8,256]{2,0,1:T(8,128)(2,1)S(1)}, u32[]{:S(2)}, u32[]{:S(2)}) async-start(bf16[192,8,256]{2,0,1:T(8,128)(2,1)} %bitcast.31), calls=%async_computation.2 | async-start | bytes 1572864 | tf_op jit(solution)/shard_map/all_to_all | solution.py:71
  272.4 2.0 copy-start.2
  580.4 1.1 copy-start.5
  580.4 1.4 copy-start.6
  584.3 16.1 %all-to-all-start = ((bf16[192,8,256]{2,0,1:T(8,128)(2,1)}), bf16[192,8,256]{2,0,1:T(8,128)(2,1)S(1)}, u32[]{:S(2)}, u32[]{:S(2)}) async-start(bf16[192,8,256]{2,0,1:T(8,128)(2,1)} %bitcast.32), calls=%async_computation | async-start | bytes 1572864 | tf_op jit(solution)/shard_map/all_to_all | solution.py:70
  600.4 0.9 copy-start.3
  966.7 420.9 %all-to-all-start.1 = ((f32[8,192,256]{2,1,0:T(8,128)}), f32[8,192,256]{2,1,0:T(8,128)}, u32[]{:S(2)}, u32[]{:S(2)}) async-start(f32[8,192,256]{2,1,0:T(8,128)} %bitcast.46), calls=%async_computation.1 | async-start | bytes 3145728 | tf_op jit(solution)/shard_map/all_to_all | solution.py:87
  970.9 414.9 %all-reduce.4.cloned.1.call-start = ((), (), s32[]{:S(2)}) async-start(), calls=%async_computation.6 | async-start | bytes 524288 | tf_op jit(solution)/shard_map/psum | solution.py:95
  1387.5 1.9 copy-start.4
  1389.2 1.3 copy-start.1
Sparse Core Ops, SparseCore 0:
  9.6 66.1 all-gather.2
  77.7 159.4 all-gather.4
  1259.6 126.2 all-reduce.3
where the time goes:
time: 1410 us; the launch traced here: 1400 us
  other arithmetic  685 us (49%)
  waiting for transfers between devices  381 us (27%)
  loops' own time  173 us (12%)
  local copies, waits for them, and re-layouts  89.3 us (6%)
  blocking collectives  23.4 us (2%)
  matrix products  19.7 us (1%)
    add x128, other arithmetic, causal_step(): return total + weight * window  363 us
    add x128, other arithmetic, anticausal_step(): return total + weight * window  278 us
    another operation x1, loops' own time, lagged(): return lax.map(one_lag, jnp.arange(prev + 1, dtype=jnp.int32))  169 us
    all_gather x1, waiting for transfers between devices, body(): panel = lax.all_gather(out_weight, 'ctx', axis=1, tiled=True)  161 us
    psum x1, waiting for transfers between devices, body(): grad_filters = lax.psum(partial_terms, ('ctx', 'mp')) * scale  126 us
    dynamic_slice x128, local copies, waits for them, and re-layouts, lagged(): return lax.map(one_lag, jnp.arange(prev + 1, dtype=jnp.int32))  75 us
    all_gather x1, waiting for transfers between devices, body(): lax.all_gather(cotangent, 'mp', axis=1, tiled=True)  67.1 us
    reduce_sum x128, other arithmetic, one_lag(): return jnp.sum(window * gradient, axis=0)  38.9 us
  transfers between devices with their start and end apart: 6, of which 5 were waited for; matrix products, arithmetic and copies ran while one was open for 9% of the time, Pallas kernels for 0%

commit v1 on v0

--- a/solution.py
+++ b/solution.py
@@ -2,6 +2,18 @@
 import jax.numpy as jnp
 from jax import lax
 from jax.sharding import PartitionSpec as P
+
+
+def doubled_up(x, axis, dim):
+    ways, here = (lax.axis_size(axis), lax.axis_index(axis))
+    grown, reach = (x, 1)
+    while reach < ways:
+        theirs = lax.ppermute(grown, axis, [(d, d ^ reach) for d in range(ways)])
+        mine_first = jnp.concatenate([grown, theirs], axis=dim)
+        theirs_first = jnp.concatenate([theirs, grown], axis=dim)
+        grown = jnp.where(here & reach == 0, mine_first, theirs_first)
+        reach = 2 * reach
+    return grown
 
 
 def causal(widened, taps, rows, prev):
@@ -62,7 +74,7 @@
     ctx_count = lax.axis_size("ctx")
     per_group = chans * lax.axis_size("mp") // groups
     panel = lax.all_gather(out_weight, "ctx", axis=1, tiled=True)
-    grad_mixed = contract(lax.all_gather(cotangent, "mp", axis=1, tiled=True), panel)
+    grad_mixed = contract(doubled_up(cotangent, "mp", 1), panel)
     product = (key_act.astype(jnp.float32) * value_act.astype(jnp.float32)).astype(jnp.bfloat16)
     grad_conv = (grad_mixed * query_act.astype(jnp.float32)).astype(jnp.bfloat16)
     narrow = chans // ctx_count

time: 1410 us -> 1340 us (0.950)
  waiting for transfers between devices: 381 us -> 309 us
    all_gather x1, waiting for transfers between devices: 161 us -> 71.9 us  [body(): panel = lax.all_gather(out_weight, 'ctx', axis=1, tiled=True)]
    ppermute x0 -> x2, waiting for transfers between devices: none -> 85.4 us  [doubled_up(): theirs = lax.ppermute(grown, axis, [(d, d ^ reach) for d in range(ways)])]
    all_gather x1 -> x0, waiting for transfers between devices: 67.1 us -> none  [body(): lax.all_gather(cotangent, 'mp', axis=1, tiled=True)]
  transfers between devices with their start and end apart: 6 -> 7, of which waited for: 5 -> 6; matrix products, arithmetic and copies ran while one was open for 9% -> 9% of each run, Pallas kernels for 0% -> 0%
where the time goes in v1:
time: 1340 us; the launch traced here: 1330 us
  other arithmetic  686 us (51%)
  waiting for transfers between devices  309 us (23%)
  loops' own time  173 us (13%)
  local copies, waits for them, and re-layouts  89.7 us (7%)
  blocking collectives  23.4 us (2%)
  matrix products  19.6 us (1%)
  starting transfers between devices  17.3 us (1%)
  between operations  14.2 us (1%)
    add x128, other arithmetic, causal_step(): return total + weight * window  362 us
    add x128, other arithmetic, anticausal_step(): return total + weight * window  277 us
    another operation x1, loops' own time, lagged(): return lax.map(one_lag, jnp.arange(prev + 1, dtype=jnp.int32))  169 us
    psum x1, waiting for transfers between devices, body(): grad_filters = lax.psum(partial_terms, ('ctx', 'mp')) * scale  126 us
    ppermute x2, waiting for transfers between devices, doubled_up(): theirs = lax.ppermute(grown, axis, [(d, d ^ reach) for d in range(ways)])  85.4 us
    dynamic_slice x128, local copies, waits for them, and re-layouts, lagged(): return lax.map(one_lag, jnp.arange(prev + 1, dtype=jnp.int32))  75 us
    all_gather x1, waiting for transfers between devices, body(): panel = lax.all_gather(out_weight, 'ctx', axis=1, tiled=True)  71.9 us
    reduce_sum x128, other arithmetic, one_lag(): return jnp.sum(window * gradient, axis=0)  38.9 us
  transfers between devices with their start and end apart: 7, of which 6 were waited for; matrix products, arithmetic and copies ran while one was open for 9% of the time, Pallas kernels for 0%

profile of v1, /device:TPU:0, one launch (start us, length us, event | category | flops | bytes accessed | tf_op | source)
XLA Modules:
  0.0 1332.3 jit_solution(13944290633413235744)
XLA Ops:
  8.4 3.0 collective-permute-start
  11.4 17.6 %collective-permute-done = bf16[192,2048]{1,0:T(8,128)(2,1)} collective-permute-done((bf16[192,2048]{1,0:T(8,128)(2,1)S(1)}, bf16[192,2048]{1,0:T(8,128)(2,1)}, u32[]{:S(2)}, u32[]{:S(2)}) %collective-permute-start) | collective-permute-done | bytes 786464 | tf_op jit(solution)/shard_map/ppermute | solution.py:11
  33.8 67.8 %collective-permute-done.1 = bf16[192,4096]{1,0:T(8,128)(2,1)} collective-permute-done((bf16[192,4096]{1,0:T(8,128)(2,1)S(1)}, bf16[192,4096]{1,0:T(8,128)(2,1)}, u32[]{:S(2)}, u32[]{:S(2)}) %collective-permute-start.1) | collective-permute-done | bytes 1572896 | tf_op jit(solution)/shard_map/ppermute | solution.py:11
  101.6 71.9 %all-gather.2.cloned.1.call-done = bf16[2048,8192]{1,0:T(8,128)(2,1)} async-done(((bf16[2048,1024]{1,0:T(8,128)(2,1)}), bf16[2048,8192]{1,0:T(8,128)(2,1)}) %all-gather.2.cloned.1.call-update) | async-done | bytes 33554448 | tf_op jit(solution)/shard_map/all_gather | solution.py:76
  173.5 17.9 %multiply_convert_fusion = (bf16[192,2048]{1,0:T(8,128)(2,1)S(1)}, f32[192,2048]{1,0:T(8,128)}) fusion(bf16[192,2048]{1,0:T(8,128)(2,1)} %param.14, bf16[2048,8192]{1,0:T(8,128)(2,1)} %all-gather.2.cloned.1.call-done, bf16[192,4096]{1,0:T(8,128)(2,1)} %collective-permute-done.1, bf16[192,4096]{1,0:T(8,128)(2,1)S(1)} %maximum_select_fusion.2, pred[]{:T(512)S(6)} %eq.19), kind=kOutput, calls=%fused_computation.20 | convolution fusion | flops 6457786368 | bytes 39845888 | tf_op jit(solution)/shard_map/dot_general | solution.py:60
  192.3 3.5 all-to-all-start.2
  196.6 11.8 all-to-all-done.2
  210.5 282.3 %while.38 = (s32[]{:T(128)}, f32[1536,256]{1,0:T(8,128)S(1)}, f32[128,256]{1,0:T(8,128)S(1)}, f32[1663,256]{1,0:T(8,128)}, s32[]{:T(128)}, /*index=5*/s32[]{:T(128)}) while((s32[]{:T(128)}, f32[1536,256]{1,0:T(8,128)S(1)}, f32[128,256]{1,0:T(8,128)S(1)}, f32[1663,256]{1,0:T(8,128)}, s32[]{:T(128)}, /*index=5*/s32[]{:T(128)}) %tuple.96), condition=%wide.region_3.4_spmd.clone, body=%wide.region_2.3_spmd.clone.sunk | while | flops 1179651 | bytes 4721751 | solution.py:41
  492.8 23.4 %all_to_all.64 = f32[8,192,256]{2,1,0:T(8,128)S(1)} all-to-all(f32[8,192,256]{2,1,0:T(8,128)S(1)} %bitcast.44), channel_id=1, replica_groups=mesh['ctx'=8,'mp'=4] {'ctx'}, dimensions={0} | all-to-all | bytes 3145728 | tf_op jit(solution)/shard_map/all_to_all | solution.py:100
  520.2 3.5 all-to-all-start
  523.7 12.5 all-to-all-done
  538.4 363.2 %while.37 = (s32[]{:T(128)}, f32[1536,256]{1,0:T(8,128)}, f32[128,256]{1,0:T(8,128)S(1)}, f32[1663,256]{1,0:T(8,128)S(1)}, s32[]{:T(128)}, /*index=5*/s32[]{:T(128)}, s32[]{:T(128)}, s32[]{:T(128)}) while((s32[]{:T(128)}, f32[1536,256]{1,0:T(8,128)}, f32[128,256]{1,0:T(8,128)S(1)}, f32[1663,256]{1,0:T(8,128)S(1)}, s32[]{:T(128)}, ...), condition=%wide.region_1.2_spmd.clone, body=%wide.region_0.1_spmd.clone.sunk | while | flops 1179655 | bytes 4721813 | solution.py:26
  540.0 2.9 select_add_fusion.4
  542.9 2.9 select_add_fusion.4
  545.7 2.9 select_add_fusion.4
  548.6 2.9 select_add_fusion.4
  551.5 2.9 select_add_fusion.4
  554.4 2.9 select_add_fusion.4
  557.3 2.9 select_add_fusion.4
  582.6 2.9 select_add_fusion.4
  585.5 2.9 select_add_fusion.4
  588.4 2.9 select_add_fusion.4
  591.3 2.9 select_add_fusion.4
  594.2 2.9 select_add_fusion.4
  597.1 2.9 select_add_fusion.4
  600.0 2.9 select_add_fusion.4
  602.9 2.9 select_add_fusion.4
  628.2 2.9 select_add_fusion.4
  631.1 2.9 select_add_fusion.4
  634.0 2.9 select_add_fusion.4
  636.9 2.9 select_add_fusion.4
  639.8 2.9 select_add_fusion.4
  642.7 2.9 select_add_fusion.4
  645.6 2.9 select_add_fusion.4
  648.5 2.9 select_add_fusion.4
  673.8 2.9 select_add_fusion.4
  676.7 2.9 select_add_fusion.4
  679.6 2.9 select_add_fusion.4
  682.5 2.9 select_add_fusion.4
  685.3 2.9 select_add_fusion.4
  688.2 2.9 select_add_fusion.4
  691.1 2.9 select_add_fusion.4
  694.0 2.9 select_add_fusion.4
  719.4 2.9 select_add_fusion.4
  725.1 2.9 select_add_fusion.4
  730.9 2.9 select_add_fusion.4
  733.8 2.9 select_add_fusion.4
  739.6 2.9 select_add_fusion.4
  764.9 2.9 select_add_fusion.4
  773.6 2.9 select_add_fusion.4
  779.4 2.9 select_add_fusion.4
  782.3 2.9 select_add_fusion.4
  813.4 2.9 select_add_fusion.4
  819.2 2.9 select_add_fusion.4
  822.1 2.9 select_add_fusion.4
  827.8 2.9 select_add_fusion.4
  830.7 2.9 select_add_fusion.4
  861.8 2.9 select_add_fusion.4
  867.6 2.9 select_add_fusion.4
  870.5 2.9 select_add_fusion.4
  876.3 2.9 select_add_fusion.4
  901.6 4.3 all-to-all-start.1
  906.0 287.3 %while.36 = (s32[]{:T(128)}, f32[128,256]{1,0:T(8,128)S(1)}, s32[128]{0:T(128)S(1)}, f32[1663,256]{1,0:T(8,128)S(1)}, f32[1536,256]{1,0:T(8,128)S(1)}, /*index=5*/s32[]{:T(128)}, s32[1]{0:T(128)}, s32[]{:T(128)}, s32[1]{0:T(128)}) while((s32[]{:T(128)}, f32[128,256]{1,0:T(8,128)S(1)}, s32[128]{0:T(128)S(1)}, f32[1663,256]{1,0:T(8,128)S(1)}, ...), condition=%wide.region_6.7_spmd, body=%wide.region_4.6_spmd.sunk | while | flops 786182 | bytes 3148959 | solution.py:56
  1194.4 126.4 %all-reduce.4.cloned.1.call-done = f32[512,128]{1,0:T(8,128)} async-done(((f32[512,128]{1,0:T(8,128)}), f32[512,128]{1,0:T(8,128)}) %all-reduce.4.cloned.1.call-update) | async-done | bytes 262160 | tf_op jit(solution)/shard_map/psum | solution.py:107
  (888 shorter events, 639.8 us)
Async XLA Ops:
  7.2 188.7 %copy-start = (f32[512,128]{1,0:T(8,128)S(1)}, f32[512,128]{1,0:T(8,128)}, u32[]{:S(2)}) copy-start(f32[512,128]{1,0:T(8,128)} %param.17) | copy-start | bytes 786436
  7.2 1.2 copy-start.5
  7.2 166.3 %all-gather.2.cloned.1.call-start = ((), (), s32[]{:S(2)}) async-start(), calls=%async_computation.4 | async-start | bytes 37748736 | tf_op jit(solution)/shard_map/all_gather | solution.py:76
  8.4 20.7 %collective-permute-start = (bf16[192,2048]{1,0:T(8,128)(2,1)S(1)}, bf16[192,2048]{1,0:T(8,128)(2,1)}, u32[]{:S(2)}, u32[]{:S(2)}) collective-permute-start(bf16[192,2048]{1,0:T(8,128)(2,1)S(1)} %copy-done.5), channel_id=1, source_target_pairs={{0,1},{1,0},{2,3},{3,2},{4,5},{5,4},{6,7},{7,6},{8,9},{9,8},{10,11... | collective-permute-start | bytes 2359304 | tf_op jit(solution)/shard_map/ppermute | solution.py:11
  31.0 70.6 %collective-permute-start.1 = (bf16[192,4096]{1,0:T(8,128)(2,1)S(1)}, bf16[192,4096]{1,0:T(8,128)(2,1)}, u32[]{:S(2)}, u32[]{:S(2)}) collective-permute-start(bf16[192,4096]{1,0:T(8,128)(2,1)S(1)} %maximum_select_fusion.2), channel_id=1, source_target_pairs={{0,2},{1,3},{2,0},{3,1},{4,6},{5,7},{6,4},{7,5},{8,10},{9,11},{10,... | collective-permute-start | bytes 4718600 | tf_op jit(solution)/shard_map/ppermute | solution.py:11
  192.3 16.1 %all-to-all-start.2 = ((bf16[192,8,256]{2,0,1:T(8,128)(2,1)}), bf16[192,8,256]{2,0,1:T(8,128)(2,1)S(1)}, u32[]{:S(2)}, u32[]{:S(2)}) async-start(bf16[192,8,256]{2,0,1:T(8,128)(2,1)} %bitcast.30), calls=%async_computation.2 | async-start | bytes 1572864 | tf_op jit(solution)/shard_map/all_to_all | solution.py:83
  208.5 2.0 copy-start.2
  516.2 1.1 copy-start.6
  516.2 1.4 copy-start.7
  520.2 16.1 %all-to-all-start = ((bf16[192,8,256]{2,0,1:T(8,128)(2,1)}), bf16[192,8,256]{2,0,1:T(8,128)(2,1)S(1)}, u32[]{:S(2)}, u32[]{:S(2)}) async-start(bf16[192,8,256]{2,0,1:T(8,128)(2,1)} %bitcast.31), calls=%async_computation | async-start | bytes 1572864 | tf_op jit(solution)/shard_map/all_to_all | solution.py:82
  536.3 0.9 copy-start.3
  901.6 420.9 %all-to-all-start.1 = ((f32[8,192,256]{2,1,0:T(8,128)}), f32[8,192,256]{2,1,0:T(8,128)}, u32[]{:S(2)}, u32[]{:S(2)}) async-start(f32[8,192,256]{2,1,0:T(8,128)} %bitcast.45), calls=%async_computation.1 | async-start | bytes 3145728 | tf_op jit(solution)/shard_map/all_to_all | solution.py:99
  905.9 414.9 %all-reduce.4.cloned.1.call-start = ((), (), s32[]{:S(2)}) async-start(), calls=%async_computation.5 | async-start | bytes 524288 | tf_op jit(solution)/shard_map/psum | solution.py:107
  1322.5 1.9 copy-start.4
  1324.2 1.3 copy-start.1
Sparse Core Ops, SparseCore 0:
  9.9 163.4 all-gather.1
  1194.5 126.2 all-reduce.3
